TPU v7x, 256 devices: a whole 4x4x8 slice. The times are simulated.
256 devices in a mesh: phase: 2 (over x_hi), ctx: 16 (over x_lo, z), head: 8 (over y, core).
Axes of the slice: x: 4 (x_hi: 2, x_lo: 2; x = x_hi * 2 + x_lo), y: 4, z: 8, core: 2. Of those that a mesh axis runs over, the one named last changes fastest.
Arguments:
- query: bfloat16 [2, 4096, 5120], P('phase', 'ctx', 'head'), may hold values from -18 to 18
- key_cache: bfloat16 [4096, 1024], P('ctx', 'head'), may hold values from -18 to 18
- value_cache: bfloat16 [4096, 1024], P('ctx', 'head'), may hold values from -6 to 6
- saved_output: bfloat16 [2, 4096, 5120], P('phase', 'ctx', 'head'), may hold values from -1.796875 to 1.796875
- out_grad: bfloat16 [2, 4096, 5120], P('phase', 'ctx', 'head'), may hold values from -6 to 6
- out_weight: bfloat16 [2, 5120, 5120], P('phase', 'head'), may hold values from -0.078125 to 0.078125
- doc_lengths: int32 [4], replicated, may hold values from 1 to 3072, 4096 in all
Outputs:
- grad_query: float32 [2, 4096, 5120], P('phase', 'ctx', 'head')
- grad_key: float32 [4096, 1024], P('ctx', 'head')
- grad_value: float32 [4096, 1024], P('ctx', 'head')
Inputs may be any that keep to these rules, and one draw needn't show every extreme that they name: `doc_lengths`: the 4 lengths sum to 4096, and one document has exactly 3072 positions.
All inputs are finite; a program needn't handle non-finite values.
Results may differ from a plain program's by a relative error of at most 0.0041.
Values may be sent and summed in bfloat16 or wider, within the bound.
No kernel may reach another device: no remote copies, remote signals or barrier semaphores. Data moves between devices by JAX's collectives and lax.ppermute only.
A program may use at most 128 MiB of HBM per device.

v0:
```python
import jax
import jax.numpy as jnp
from jax import lax
from jax.sharding import PartitionSpec as P

HD = 128
BLOCK = 512
MASKED = -1e30


def segment_of(places, ends):
    return jnp.sum((places[:, None] >= ends[None, :]).astype(jnp.int32), axis=1)


def visible(query_place, query_segment, key_place, key_segment):
    return (key_place[None, :] <= query_place[:, None]) & (
        key_segment[None, :] == query_segment[:, None]
    )


def block_scores(queries, keys, allowed, scale):
    scores = jnp.einsum("tjgd,kjd->jgtk", queries, keys, preferred_element_type=jnp.float32) * scale
    return jnp.where(allowed[None, None], scores, MASKED)


def running_update(carry, scores, allowed):
    largest, total = carry
    raised = jnp.maximum(largest, jnp.max(scores, axis=-1))
    terms = jnp.where(allowed[None, None], jnp.exp(scores - raised[..., None]), 0.0)
    return (raised, total * jnp.exp(largest - raised) + jnp.sum(terms, axis=-1))


def block_grads(queries, grads, keys, values, allowed, log_total, delta, scale):
    scores = block_scores(queries, keys, allowed, scale)
    weights = jnp.where(allowed[None, None], jnp.exp(scores - log_total[..., None]), 0.0)
    weights_low = weights.astype(jnp.bfloat16)
    value_grad = jnp.einsum(
        "jgtk,tjgd->kjd", weights_low, grads, preferred_element_type=jnp.float32
    )
    weight_grad = jnp.einsum("tjgd,kjd->jgtk", grads, values, preferred_element_type=jnp.float32)
    score_grad = (weights * (weight_grad - delta[..., None])).astype(jnp.bfloat16)
    query_grad = jnp.einsum("jgtk,kjd->tjgd", score_grad, keys, preferred_element_type=jnp.float32)
    key_grad = jnp.einsum("jgtk,tjgd->kjd", score_grad, queries, preferred_element_type=jnp.float32)
    return (query_grad, key_grad, value_grad)


def body(query, key_cache, value_cache, saved_output, out_grad, out_weight, doc_lengths):
    rows = query.shape[1]
    query_cols = query.shape[2]
    key_cols = key_cache.shape[1]
    kv_heads = key_cols // HD
    groups = query_cols // key_cols
    scale = HD ** (-0.5)
    rank = lax.axis_index("ctx")
    ends = jnp.cumsum(doc_lengths)
    query_place = rank * rows + jnp.arange(rows, dtype=jnp.int32)
    query_segment = segment_of(query_place, ends)
    grad_rows = out_grad[0]
    weight = out_weight[0]
    grad_attn = lax.psum_scatter(
        lax.dot_general(
            weight, grad_rows, (((0,), (1,)), ((), ())), preferred_element_type=jnp.float32
        ),
        "head",
        scatter_dimension=0,
        tiled=True,
    ).T.astype(jnp.bfloat16)
    queries = query[0].reshape(rows, kv_heads, groups, HD)
    grads = grad_attn.reshape(rows, kv_heads, groups, HD)
    outputs = saved_output[0].reshape(rows, kv_heads, groups, HD)
    delta = jnp.einsum("tjgd,tjgd->jgt", grads, outputs, preferred_element_type=jnp.float32)
    initial = (
        jnp.full((kv_heads, groups, rows), MASKED, jnp.float32),
        jnp.zeros((kv_heads, groups, rows), jnp.float32),
    )
    whole_keys, whole_values = (
        lax.all_gather(key_cache, "ctx", axis=0, tiled=True),
        lax.all_gather(value_cache, "ctx", axis=0, tiled=True),
    )
    length = whole_keys.shape[0]
    parts = length // BLOCK
    key_blocks = whole_keys.reshape(parts, BLOCK, kv_heads, HD)
    value_blocks = whole_values.reshape(parts, BLOCK, kv_heads, HD)
    key_places = jnp.arange(length, dtype=jnp.int32)
    key_segments = segment_of(key_places, ends).reshape(parts, BLOCK)
    key_places = key_places.reshape(parts, BLOCK)

    def stats_step(carry, inputs):
        keys, places, segments = inputs
        allowed = visible(query_place, query_segment, places, segments)
        return (running_update(carry, block_scores(queries, keys, allowed, scale), allowed), None)

    (largest, total), _ = lax.scan(stats_step, initial, (key_blocks, key_places, key_segments))
    log_total = largest + jnp.log(total)

    def grad_step(carry, inputs):
        keys, values, places, segments = inputs
        allowed = visible(query_place, query_segment, places, segments)
        query_grad, key_grad, value_grad = block_grads(
            queries, grads, keys, values, allowed, log_total, delta, scale
        )
        joined = jnp.concatenate(
            [key_grad.reshape(BLOCK, key_cols), value_grad.reshape(BLOCK, key_cols)], axis=1
        )
        return (carry + query_grad, joined)

    query_sum, kv_terms = lax.scan(
        grad_step,
        jnp.zeros((rows, kv_heads, groups, HD), jnp.float32),
        (key_blocks, value_blocks, key_places, key_segments),
    )
    mine = lax.psum_scatter(
        kv_terms.reshape(length, 2 * key_cols), "ctx", scatter_dimension=0, tiled=True
    )
    key_sum = mine[:, :key_cols] * scale
    value_sum = mine[:, key_cols:]
    query_sum = query_sum.reshape(rows, query_cols)
    key_total, value_total = lax.psum((key_sum, value_sum), "phase")
    grad_query = (query_sum * scale).reshape(1, rows, query_cols)
    return (grad_query, key_total, value_total)


def solution(mesh):
    placed = (
        P("phase", "ctx", "head"),
        P("ctx", "head"),
        P("ctx", "head"),
        P("phase", "ctx", "head"),
        P("phase", "ctx", "head"),
        P("phase", "head", None),
        P(),
    )
    return jax.shard_map(
        body,
        mesh=mesh,
        in_specs=placed,
        out_specs=(P("phase", "ctx", "head"), P("ctx", "head"), P("ctx", "head")),
        check_vma=False,
    )
```

profile of v0, /device:TPU:1, one launch (start us, length us, event | category | flops | bytes accessed | tf_op | source)
XLA Modules:
  0.0 339.7 jit_solution(13072499944512161214)
XLA Ops:
  9.0 7.4 %fusion.42 = f32[5120,256]{1,0:T(8,128)} fusion(bf16[1,640,5120]{2,1,0:T(8,128)(2,1)} %param.16, bf16[1,256,640]{2,1,0:T(8,128)(2,1)S(1)} %copy-done), kind=kOutput, calls=%fused_computation.56 | convolution fusion | flops 1677721600 | bytes 12124160 | tf_op jit(solution)/shard_map/dot_general | solution.py:61
  17.9 0.9 copy.38
  18.8 0.9 copy.55
  19.7 52.7 %all-gather.3.cloned.1.call-done = bf16[4096,128]{1,0:T(8,128)(2,1)} async-done(((bf16[256,128]{1,0:T(8,128)(2,1)}), bf16[4096,128]{1,0:T(8,128)(2,1)}) %all-gather.3.cloned.1.call-update) | async-done | bytes 1048592 | tf_op jit(solution)/shard_map/all_gather | solution.py:77
  72.4 20.6 %while.26 = (s32[]{:T(128)}, f32[1,5,256]{2,1,0:T(8,128)S(1)}, f32[1,5,256]{2,1,0:T(8,128)S(1)}, s32[8,512]{1,0:T(8,128)S(1)}, s32[8,512]{1,0:T(8,128)S(1)}, /*i...) while((s32[]{:T(128)}, f32[1,5,256]{2,1,0:T(8,128)S(1)}, ...), condition=%wide.region_6.7_spmd.clone, body=%wide.region_3.0_spmd.clone.sunk | while | flops 173414912 | bytes 6176908 | solution.py:93
  72.7 1.6 fusion.64
  75.2 1.6 fusion.64
  77.8 1.6 fusion.64
  80.4 1.6 fusion.64
  83.0 1.6 fusion.64
  85.6 1.6 fusion.64
  88.1 1.6 fusion.64
  90.7 1.6 fusion.64
  93.1 1.1 convert_element_type.20
  94.2 1.1 fusion.44
  95.3 45.4 %all-gather.5.cloned.1.call-done = bf16[4096,128]{1,0:T(8,128)(2,1)} async-done(((bf16[256,128]{1,0:T(8,128)(2,1)}), bf16[4096,128]{1,0:T(8,128)(2,1)}) %all-gather.5.cloned.1.call-update) | async-done | bytes 1048592 | tf_op jit(solution)/shard_map/all_gather | solution.py:78
  140.8 65.1 %while.27 = (s32[]{:T(128)}, f32[256,1,5,128]{0,3,2,1:T(8,128)}, f32[8,512,256]{2,1,0:T(8,128)}, bf16[8,512,1,128]{3,1,2,0:T(8,128)(2,1)}, s32[8,512]{1,0:T(8,12...) while((s32[]{:T(128)}, f32[256,1,5,128]{0,3,2,1:T(8,128)}, ...), condition=%wide.region_9.10_spmd.clone, body=%wide.region_8.9_spmd.clone.sunk | while | flops 847577344 | bytes 45119780 | solution.py:107
  140.8 1.4 fusion.75
  142.4 2.1 fusion.76
  144.6 1.5 fusion.77
  148.9 1.4 fusion.75
  150.5 2.1 fusion.76
  152.7 1.5 fusion.77
  157.0 1.4 fusion.75
  158.7 2.1 fusion.76
  160.8 1.5 fusion.77
  165.1 1.4 fusion.75
  166.8 2.1 fusion.76
  168.9 1.5 fusion.77
  173.3 1.4 fusion.75
  174.9 2.1 fusion.76
  177.1 1.5 fusion.77
  181.4 1.4 fusion.75
  183.0 2.1 fusion.76
  185.2 1.5 fusion.77
  188.7 0.9 constant_dynamic-update-slice_fusion.2
  189.5 1.4 fusion.75
  191.2 2.1 fusion.76
  193.3 1.5 fusion.77
  197.7 1.4 fusion.75
  199.3 2.1 fusion.76
  201.5 1.5 fusion.77
  205.9 78.6 %reduce-scatter.5.cloned.1.call-done = f32[256,256]{1,0:T(8,128)} async-done(((f32[4096,256]{1,0:T(8,128)}), f32[256,256]{1,0:T(8,128)}) %reduce-scatter.5.cloned.1.call-update) | async-done | bytes 262160 | tf_op jit(solution)/shard_map/reduce_scatter | solution.py:112
  284.5 1.7 fusion.46
  286.3 1.1 copy.41
  287.3 42.1 %all-reduce.3.cloned.1.call-done = (f32[256,128]{1,0:T(8,128)}, f32[256,128]{1,0:T(8,128)}) async-done(((f32[256,128]{1,0:T(8,128)}, f32[256,128]{1,0:T(8,128)}), (f32[256,128]{1,0:T(8,128)}, f32[256,128]{1,0:T(8,128)})) %all-reduce.3.cloned.1.call-update) | async-done | bytes 262160 | tf_op jit(solution)/shard_map/psum | solution.py:118
  329.5 1.6 copy.82
  331.1 1.6 copy.83
  (217 shorter events, 32.7 us)
Async XLA Ops:
  8.0 1.0 copy-start
  8.0 64.4 %all-gather.3.cloned.1.call-start = ((), (), s32[]{:S(2)}) async-start(), calls=%async_computation.2 | async-start | bytes 1114112 | tf_op jit(solution)/shard_map/all_gather | solution.py:77
  8.7 84.3 %reduce-scatter.3.cloned.1.call-start = ((), (), s32[]{:S(2)}) async-start(), calls=%async_computation.4 | async-start | bytes 5898240 | tf_op jit(solution)/shard_map/reduce_scatter | solution.py:60
  16.4 0.9 copy-start.8
  16.4 1.3 copy-start.6
  16.4 2.4 copy-start.7
  16.4 124.3 %all-gather.5.cloned.1.call-start = ((), (), s32[]{:S(2)}) async-start(), calls=%async_computation.3 | async-start | bytes 1114112 | tf_op jit(solution)/shard_map/all_gather | solution.py:78
  17.2 267.3 %reduce-scatter.5.cloned.1.call-start = ((), (), s32[]{:S(2)}) async-start(), calls=%async_computation.5 | async-start | bytes 4456448 | tf_op jit(solution)/shard_map/reduce_scatter | solution.py:112
  142.1 2.4 copy-start.1
  142.4 2.2 copy-start.3
  144.6 1.8 copy-start.2
  146.1 1.1 copy-start.4
  150.3 2.4 copy-start.1
  150.5 2.2 copy-start.3
  152.7 1.8 copy-start.2
  154.2 1.1 copy-start.4
  158.4 2.4 copy-start.1
  158.6 2.2 copy-start.3
  160.8 1.8 copy-start.2
  162.3 1.1 copy-start.4
  166.5 2.4 copy-start.1
  166.8 2.2 copy-start.3
  168.9 1.8 copy-start.2
  170.5 1.1 copy-start.4
  174.7 2.4 copy-start.1
  174.9 2.2 copy-start.3
  177.1 1.8 copy-start.2
  178.6 1.1 copy-start.4
  182.8 2.4 copy-start.1
  183.0 2.2 copy-start.3
  185.2 1.8 copy-start.2
  186.7 1.1 copy-start.4
  190.9 2.4 copy-start.1
  191.2 2.1 copy-start.3
  193.3 1.8 copy-start.2
  194.9 1.1 copy-start.4
  199.1 2.4 copy-start.1
  199.3 2.1 copy-start.3
  201.5 1.8 copy-start.2
  203.0 1.1 copy-start.4
  205.8 80.3 %copy-start.5 = (f32[256,1,5,128]{0,3,2,1:T(8,128)S(1)}, f32[256,1,5,128]{0,3,2,1:T(8,128)}, u32[]{:S(2)}) copy-start(f32[256,1,5,128]{0,3,2,1:T(8,128)} %get-tuple-element.121) | copy-start | bytes 1966084
  205.9 123.6 %all-reduce.3.cloned.1.call-start = ((), (), s32[]{:S(2)}) async-start(), calls=%async_computation.6 | async-start | bytes 524288 | tf_op jit(solution)/shard_map/psum | solution.py:118
Sparse Core Ops, SparseCore 0:
  10.6 61.7 all-gather.2
  74.2 66.5 all-gather.4
  206.0 78.4 reduce-scatter.4
Sparse Core Ops, SparseCore 1:
  16.5 44.4 reduce-scatter.2
  286.3 43.2 all-reduce.2
where the time goes:
time: 341 us; the launch traced here: 340 us
  waiting for transfers between devices  220 us (65%)
  matrix products  71.6 us (21%)
  local copies, waits for them, and re-layouts  17.3 us (5%)
  between operations  15.3 us (4%)
  other arithmetic  13.3 us (4%)
    reduce_scatter x1, waiting for transfers between devices, body(): lax.psum_scatter(kv_terms.reshape(length, 2 * key_cols), 'ctx', scatter_d...  78.6 us
    all_gather x1, waiting for transfers between devices, body(): lax.all_gather(key_cache, 'ctx', axis=0, tiled=True)  52.7 us
    all_gather x1, waiting for transfers between devices, body(): lax.all_gather(value_cache, 'ctx', axis=0, tiled=True)  45.4 us
    psum x1, waiting for transfers between devices, body(): key_total, value_total = lax.psum((key_sum, value_sum), 'phase')  42.1 us
    dot_general x16, matrix products, block_scores(): jnp.einsum('tjgd,kjd->jgtk', queries, keys, preferred_element_type=jnp.fl...  24 us
    dot_general x8, matrix products, block_grads(): jnp.einsum('tjgd,kjd->jgtk', grads, values, preferred_element_type=jnp.fl...  16.9 us
    dot_general x8, matrix products, block_grads(): jnp.einsum('jgtk,kjd->tjgd', score_grad, keys, preferred_element_type=jnp...  12 us
    dynamic_update_slice x16, local copies, waits for them, and re-layouts, body(): lax.scan(grad_step, jnp.zeros((rows, kv_heads, groups, HD), jnp.float32),...  8.37 us
  transfers between devices with their start and end apart: 5, of which 4 were waited for; matrix products, arithmetic and copies ran while one was open for 10% of the time, Pallas kernels for 0%

commit v1 on v0

--- a/solution.py
+++ b/solution.py
@@ -75,7 +75,9 @@
     )
     whole_keys, whole_values = (
         lax.all_gather(key_cache, "ctx", axis=0, tiled=True),
-        lax.all_gather(value_cache, "ctx", axis=0, tiled=True),
+        jnp.concatenate(
+            lax.all_to_all(jnp.stack([value_cache] * lax.axis_size("ctx")), "ctx", 0, 0), axis=0
+        ),
     )
     length = whole_keys.shape[0]
     parts = length // BLOCK

time: 341 us -> 303 us (0.89)
  waiting for transfers between devices: 220 us -> 169 us
  starting transfers between devices: 0.2 us -> 10.3 us
    all_gather x1 -> x0, waiting for transfers between devices: 45.4 us -> none  [body(): lax.all_gather(value_cache, 'ctx', axis=0, tiled=True)]
    all_to_all x0 -> x1, starting transfers between devices: none -> 10.1 us  [body(): lax.all_to_all(jnp.stack([value_cache] * lax.axis_size('ctx')), 'ctx', 0, 0)]
    all_gather x1, waiting for transfers between devices: 52.7 us -> 48 us  [body(): lax.all_gather(key_cache, 'ctx', axis=0, tiled=True)]
  transfers between devices with their start and end apart: 5 -> 5, of which waited for: 4 -> 3; matrix products, arithmetic and copies ran while one was open for 10% -> 12% of each run, Pallas kernels for 0% -> 0%
where the time goes in v1:
time: 303 us; the launch traced here: 301 us
  waiting for transfers between devices  169 us (56%)
  matrix products  71.6 us (24%)
  local copies, waits for them, and re-layouts  19.7 us (7%)
  between operations  15.3 us (5%)
  other arithmetic  13.2 us (4%)
  starting transfers between devices  10.3 us (3%)
    reduce_scatter x1, waiting for transfers between devices, body(): lax.psum_scatter(kv_terms.reshape(length, 2 * key_cols), 'ctx', scatter_d...  77 us
    all_gather x1, waiting for transfers between devices, body(): lax.all_gather(key_cache, 'ctx', axis=0, tiled=True)  48 us
    psum x1, waiting for transfers between devices, body(): key_total, value_total = lax.psum((key_sum, value_sum), 'phase')  43.7 us
    dot_general x16, matrix products, block_scores(): jnp.einsum('tjgd,kjd->jgtk', queries, keys, preferred_element_type=jnp.fl...  24 us
    dot_general x8, matrix products, block_grads(): jnp.einsum('tjgd,kjd->jgtk', grads, values, preferred_element_type=jnp.fl...  16.9 us
    dot_general x8, matrix products, block_grads(): jnp.einsum('jgtk,kjd->tjgd', score_grad, keys, preferred_element_type=jnp...  12 us
    all_to_all x1, starting transfers between devices, body(): lax.all_to_all(jnp.stack([value_cache] * lax.axis_size('ctx')), 'ctx', 0, 0)  10.1 us
    dynamic_update_slice x16, local copies, waits for them, and re-layouts, body(): lax.scan(grad_step, jnp.zeros((rows, kv_heads, groups, HD), jnp.float32),...  8.41 us
  transfers between devices with their start and end apart: 5, of which 3 were waited for; matrix products, arithmetic and copies ran while one was open for 12% of the time, Pallas kernels for 0%

profile of v1, /device:TPU:1, one launch (start us, length us, event | category | flops | bytes accessed | tf_op | source)
XLA Modules:
  0.0 301.3 jit_solution(14199291682239048921)
XLA Ops:
  8.7 2.0 stack.2
  10.8 10.1 %all-to-all-start = ((bf16[16,256,128]{2,1,0:T(8,128)(2,1)}), bf16[16,256,128]{2,1,0:T(8,128)(2,1)}, u32[]{:S(2)}, u32[]{:S(2)}) async-start(bf16[16,256,128]{2,1,0:T(8,128)(2,1)} %stack.2), calls=%async_computation | async-start | bytes 2097152 | tf_op jit(solution)/shard_map/all_to_all | solution.py:79
  20.9 7.4 %fusion.42 = f32[5120,256]{1,0:T(8,128)} fusion(bf16[1,640,5120]{2,1,0:T(8,128)(2,1)} %param.16, bf16[1,256,640]{2,1,0:T(8,128)(2,1)S(1)} %copy-done), kind=kOutput, calls=%fused_computation.56 | convolution fusion | flops 1677721600 | bytes 12124160 | tf_op jit(solution)/shard_map/dot_general | solution.py:61
  29.6 0.9 copy.38
  30.5 0.9 copy.55
  31.4 48.0 %all-gather.2.cloned.1.call-done = bf16[4096,128]{1,0:T(8,128)(2,1)} async-done(((bf16[256,128]{1,0:T(8,128)(2,1)}), bf16[4096,128]{1,0:T(8,128)(2,1)}) %all-gather.2.cloned.1.call-update) | async-done | bytes 1048592 | tf_op jit(solution)/shard_map/all_gather | solution.py:77
  79.4 20.6 %while.26 = (s32[]{:T(128)}, f32[1,5,256]{2,1,0:T(8,128)S(1)}, f32[1,5,256]{2,1,0:T(8,128)S(1)}, s32[8,512]{1,0:T(8,128)S(1)}, s32[8,512]{1,0:T(8,128)S(1)}, /*i...) while((s32[]{:T(128)}, f32[1,5,256]{2,1,0:T(8,128)S(1)}, ...), condition=%wide.region_6.7_spmd.clone, body=%wide.region_3.0_spmd.clone.sunk | while | flops 173414912 | bytes 6176908 | solution.py:95
  79.6 1.6 fusion.64
  82.2 1.6 fusion.64
  84.8 1.6 fusion.64
  87.4 1.6 fusion.64
  89.9 1.6 fusion.64
  92.5 1.6 fusion.64
  95.1 1.6 fusion.64
  97.7 1.6 fusion.64
  100.1 1.1 convert_element_type.20
  101.2 1.1 fusion.44
  102.3 65.1 %while.27 = (s32[]{:T(128)}, f32[256,1,5,128]{0,3,2,1:T(8,128)}, f32[8,512,256]{2,1,0:T(8,128)}, bf16[8,512,1,128]{3,1,2,0:T(8,128)(2,1)}, s32[8,512]{1,0:T(8,12...) while((s32[]{:T(128)}, f32[256,1,5,128]{0,3,2,1:T(8,128)}, ...), condition=%wide.region_9.10_spmd.clone, body=%wide.region_8.9_spmd.clone.sunk | while | flops 847577344 | bytes 45119780 | solution.py:109
  102.3 1.4 fusion.75
  103.9 2.1 fusion.76
  106.1 1.5 fusion.77
  110.4 1.4 fusion.75
  112.1 2.1 fusion.76
  114.2 1.5 fusion.77
  118.5 1.4 fusion.75
  120.2 2.1 fusion.76
  122.4 1.5 fusion.77
  126.7 1.4 fusion.75
  128.3 2.1 fusion.76
  130.5 1.5 fusion.77
  134.8 1.4 fusion.75
  136.5 2.1 fusion.76
  138.6 1.5 fusion.77
  142.9 1.4 fusion.75
  144.6 2.1 fusion.76
  146.7 1.5 fusion.77
  151.1 1.4 fusion.75
  152.7 2.1 fusion.76
  154.9 1.5 fusion.77
  159.2 1.4 fusion.75
  160.9 2.1 fusion.76
  163.1 1.5 fusion.77
  167.5 77.0 %reduce-scatter.5.cloned.1.call-done = f32[256,256]{1,0:T(8,128)} async-done(((f32[4096,256]{1,0:T(8,128)}), f32[256,256]{1,0:T(8,128)}) %reduce-scatter.5.cloned.1.call-update) | async-done | bytes 262160 | tf_op jit(solution)/shard_map/reduce_scatter | solution.py:114
  244.5 1.7 fusion.46
  246.3 1.1 copy.41
  247.4 43.7 %all-reduce.3.cloned.1.call-done = (f32[256,128]{1,0:T(8,128)}, f32[256,128]{1,0:T(8,128)}) async-done(((f32[256,128]{1,0:T(8,128)}, f32[256,128]{1,0:T(8,128)}), (f32[256,128]{1,0:T(8,128)}, f32[256,128]{1,0:T(8,128)})) %all-reduce.3.cloned.1.call-update) | async-done | bytes 262160 | tf_op jit(solution)/shard_map/psum | solution.py:120
  291.0 1.6 copy.82
  292.6 1.6 copy.83
  (217 shorter events, 33.2 us)
Async XLA Ops:
  8.0 12.9 %copy-start = (bf16[1,256,640]{2,1,0:T(8,128)(2,1)S(1)}, bf16[1,256,640]{2,1,0:T(8,128)(2,1)}, u32[]{:S(2)}) copy-start(bf16[1,256,640]{2,1,0:T(8,128)(2,1)} %param.15) | copy-start | bytes 983044
  8.0 71.4 %all-gather.2.cloned.1.call-start = ((), (), s32[]{:S(2)}) async-start(), calls=%async_computation.3 | async-start | bytes 1114112 | tf_op jit(solution)/shard_map/all_gather | solution.py:77
  10.8 91.5 %all-to-all-start = ((bf16[16,256,128]{2,1,0:T(8,128)(2,1)}), bf16[16,256,128]{2,1,0:T(8,128)(2,1)}, u32[]{:S(2)}, u32[]{:S(2)}) async-start(bf16[16,256,128]{2,1,0:T(8,128)(2,1)} %stack.2), calls=%async_computation | async-start | bytes 2097152 | tf_op jit(solution)/shard_map/all_to_all | solution.py:79
  20.9 79.2 %reduce-scatter.3.cloned.1.call-start = ((), (), s32[]{:S(2)}) async-start(), calls=%async_computation.4 | async-start | bytes 5898240 | tf_op jit(solution)/shard_map/reduce_scatter | solution.py:60
  28.3 0.7 copy-start.8
  28.3 1.1 copy-start.6
  28.4 2.1 copy-start.7
  28.4 216.1 %reduce-scatter.5.cloned.1.call-start = ((), (), s32[]{:S(2)}) async-start(), calls=%async_computation.5 | async-start | bytes 4456448 | tf_op jit(solution)/shard_map/reduce_scatter | solution.py:114
  103.7 2.4 copy-start.1
  103.9 2.1 copy-start.3
  106.1 1.8 copy-start.2
  107.6 1.1 copy-start.4
  111.8 2.4 copy-start.1
  112.1 2.2 copy-start.3
  114.2 1.8 copy-start.2
  115.7 1.1 copy-start.4
  119.9 2.4 copy-start.1
  120.2 2.2 copy-start.3
  122.3 1.8 copy-start.2
  123.9 1.1 copy-start.4
  128.1 2.4 copy-start.1
  128.3 2.2 copy-start.3
  130.5 1.8 copy-start.2
  132.0 1.1 copy-start.4
  136.2 2.4 copy-start.1
  136.5 2.2 copy-start.3
  138.6 1.8 copy-start.2
  140.1 1.1 copy-start.4
  144.3 2.4 copy-start.1
  144.6 2.1 copy-start.3
  146.7 1.8 copy-start.2
  148.2 1.1 copy-start.4
  152.5 2.4 copy-start.1
  152.7 2.2 copy-start.3
  154.9 1.8 copy-start.2
  156.4 1.1 copy-start.4
  160.6 2.4 copy-start.1
  160.9 2.2 copy-start.3
  163.0 1.8 copy-start.2
  164.6 1.1 copy-start.4
  167.4 78.8 %copy-start.5 = (f32[256,1,5,128]{0,3,2,1:T(8,128)S(1)}, f32[256,1,5,128]{0,3,2,1:T(8,128)}, u32[]{:S(2)}) copy-start(f32[256,1,5,128]{0,3,2,1:T(8,128)} %get-tuple-element.121) | copy-start | bytes 1966084
  167.4 123.6 %all-reduce.3.cloned.1.call-start = ((), (), s32[]{:S(2)}) async-start(), calls=%async_computation.6 | async-start | bytes 524288 | tf_op jit(solution)/shard_map/psum | solution.py:120
Sparse Core Ops, SparseCore 0:
  10.6 68.7 all-gather.1
  167.6 76.9 reduce-scatter.4
  247.7 43.2 all-reduce.2
Sparse Core Ops, SparseCore 1:
  28.5 42.6 reduce-scatter.2
